TPU v7x, 256 devices: a whole 4x4x8 slice. The times are simulated.
256 devices in a mesh: seq: 64 (over z, y, x_lo), head: 4 (over x_hi, core).
Axes of the slice: x: 4 (x_hi: 2, x_lo: 2; x = x_hi * 2 + x_lo), y: 4, z: 8, core: 2. Of those that a mesh axis runs over, the one named last changes fastest.
Arguments:
- features: bfloat16 [8192, 960], P('seq', 'head'), may hold values from -36 to 36
- conv_weight: bfloat16 [960, 120, 128], P('head'), may hold values from -0.046875 to 0.046875
- ln_gain: float32 [960], replicated, may hold values from 0.5 to 1.5
- ln_bias: float32 [960], replicated, may hold values from -4 to 4
- query_weight: bfloat16 [8, 115200], P('head'), may hold values from -0.875 to 0.875
- key_weight: bfloat16 [8, 115200], P('head'), may hold values from -0.875 to 0.875
- value_weight: bfloat16 [8, 115200], P('head'), may hold values from -0.1875 to 0.1875
- out_weight: bfloat16 [960, 960], P('head'), may hold values from -0.1875 to 0.1875
- proj_weight: bfloat16 [960, 1024], P(None, 'head'), may hold values from -0.10085894 to 0.10085894
- targets: bfloat16 [8192, 1024], P('seq', 'head'), may hold values from -3.125 to 3.125
- mask_positions: int32 [1024], P('seq'), may hold values from 0 to 8191, as said below
- distractors: int32 [1024, 100], P('seq'), may hold values from 0 to 8191, as said below
- loss_weight: float32 [1024], P('seq'), may hold values from 0.2 to 2
Outputs:
- encoded: bfloat16 [8192, 960], P('seq', 'head')
- proj_grad: float32 [960, 1024], P(None, 'head')
- target_grad: float32 [8192, 1024], P('seq', 'head')
Inputs may be any that keep to these rules, and one draw needn't show every extreme that they name: `mask_positions`: the entries of aligned block d of 16 are distinct frames of d * 128 to (d + 1) * 128 - 1. `distractors`: call value // 128 the block of an entry. In every aligned block of 16 rows exactly 50 entries name one block, the same block for all row blocks and drawn from the seed; the remaining 16 * 100 - 50 entries of the row block are spread over the other blocks as evenly as possible.
All inputs are finite; a program needn't handle non-finite values.
Results may differ from a plain program's by a relative error of at most 0.007.
Values may be sent and summed in bfloat16 or wider, within the bound.
No kernel may reach another device: no remote copies, remote signals or barrier semaphores. Data moves between devices by JAX's collectives and lax.ppermute only.
A program may use at most 128 MiB of HBM per device.

v0:
```python
import math
import jax
import jax.numpy as jnp
from jax import lax
from jax.sharding import PartitionSpec as P

TAPS = 128
NORM_EPS = 1e-05
EPSILON = 1e-06
SOFTMAX_WARMTH = 0.1


def with_halo(shard, sides, width):
    for axis, dim in sides:
        size, length = (lax.axis_size(axis), shard.shape[dim])
        up = [(i, (i + 1) % size) for i in range(size - 1)]
        down = [(j, i) for i, j in up]
        last = lax.slice_in_dim(shard, length - width, length, axis=dim)
        first = lax.slice_in_dim(shard, 0, width, axis=dim)
        before = lax.ppermute(last, axis, up)
        after = lax.ppermute(first, axis, down)
        shard = jnp.concatenate([before, shard, after], axis=dim)
    return shard


def layer_norm(hidden, gain_terms, bias_terms):
    wide = hidden.astype(jnp.float32)
    center = jnp.mean(wide, axis=-1, keepdims=True)
    spread = jnp.mean((wide - center) ** 2, axis=-1, keepdims=True)
    return ((wide - center) * lax.rsqrt(spread + NORM_EPS) * gain_terms + bias_terms).astype(
        jnp.bfloat16
    )


def head_project(normed, flat_weight, head_count, head_dim):
    full_width = normed.shape[1]
    head_weight = flat_weight.reshape(head_count, full_width, head_dim)
    result = jnp.einsum("tw,hwd->thd", normed, head_weight, preferred_element_type=jnp.float32)
    return result.astype(jnp.bfloat16)


def contrast_terms(products, target_sq, context_sq, weight_matrix):
    inv_context = lax.rsqrt(context_sq + EPSILON)
    inv_target = lax.rsqrt(target_sq + EPSILON)
    cosine_scores = products * inv_context[:, None] * inv_target
    exponentiated = jnp.exp(cosine_scores / SOFTMAX_WARMTH)
    softmax_shares = exponentiated / jnp.sum(exponentiated, axis=1, keepdims=True)
    leading_term = (lax.broadcasted_iota(jnp.int32, softmax_shares.shape, 1) == 0).astype(
        jnp.float32
    )
    logit_slope = weight_matrix[:, None] * (softmax_shares - leading_term) / SOFTMAX_WARMTH
    along = logit_slope * inv_context[:, None] * inv_target
    shrink = logit_slope * cosine_scores * inv_target * inv_target
    spread = jnp.sum(logit_slope * cosine_scores, axis=1) * inv_context * inv_context
    return (along, shrink, spread)


def attend_block(running, key_block, value_block, query_heads, head_count, score_scale):
    numer, denom, highest = running
    row_count = key_block.shape[0]
    key_heads = key_block.reshape(row_count, head_count, -1)
    value_heads = value_block.reshape(row_count, head_count, -1)
    scores = (
        jnp.einsum("qhd,khd->hqk", query_heads, key_heads, preferred_element_type=jnp.float32)
        * score_scale
    )
    new_high = jnp.maximum(highest, jnp.max(scores, axis=2))
    factor = jnp.exp(highest - new_high)
    weights = jnp.exp(scores - new_high[:, :, None])
    denom = denom * factor + jnp.sum(weights, axis=2)
    numer = numer * factor[:, :, None] + jnp.einsum(
        "hqk,khd->hqd",
        weights.astype(jnp.bfloat16),
        value_heads,
        preferred_element_type=jnp.float32,
    )
    return (numer, denom, new_high)


def take_rows(asked, targets):
    return targets[jnp.maximum(asked, 0)]


def place_rows(asked_flat, rows_flat, frame_count):
    segment_ids = jnp.where(asked_flat >= 0, asked_flat, frame_count)
    return jax.ops.segment_sum(rows_flat, segment_ids, num_segments=frame_count + 1)[:frame_count]


def per_device(
    features,
    conv_weight,
    ln_gain,
    ln_bias,
    query_weight,
    key_weight,
    value_weight,
    out_weight,
    proj_weight,
    targets,
    mask_positions,
    distractors,
    loss_weight,
):
    frame_count, local_width = features.shape
    head_dim = conv_weight.shape[1]
    head_count = local_width // head_dim
    extended = with_halo(features, (("seq", 0),), TAPS // 2)
    position = lax.conv_general_dilated(
        extended[None],
        conv_weight,
        (1,),
        "VALID",
        dimension_numbers=("NWC", "OIW", "NWC"),
        feature_group_count=head_count,
        preferred_element_type=jnp.float32,
    )[0, :frame_count]
    hidden = (features.astype(jnp.float32) + jax.nn.gelu(position, approximate=False)).astype(
        jnp.bfloat16
    )
    normed = layer_norm(lax.all_gather(hidden, "head", axis=1, tiled=True), ln_gain, ln_bias)
    query_heads = head_project(normed, query_weight, head_count, head_dim)
    key_here = head_project(normed, key_weight, head_count, head_dim).reshape(
        frame_count, local_width
    )
    value_here = head_project(normed, value_weight, head_count, head_dim).reshape(
        frame_count, local_width
    )
    score_scale = 1.0 / math.sqrt(head_dim)
    initial = (
        jnp.zeros((head_count, frame_count, head_dim), jnp.float32),
        jnp.zeros((head_count, frame_count), jnp.float32),
        jnp.full((head_count, frame_count), -1e30, jnp.float32),
    )
    running = initial
    key_piece = lax.all_gather(key_here, "seq", axis=0, tiled=True)
    value_piece = lax.all_gather(value_here, "seq", axis=0, tiled=True)
    row_count = key_piece.shape[0]

    def advance(partial_value, blocks):
        return (
            attend_block(partial_value, blocks[0], blocks[1], query_heads, head_count, score_scale),
            None,
        )

    running, _ = lax.scan(
        advance,
        running,
        (
            key_piece.reshape(row_count // 512, 512, -1),
            value_piece.reshape(row_count // 512, 512, -1),
        ),
    )
    numer, denom, _ = running
    attended = (
        (numer / denom[:, :, None])
        .astype(jnp.bfloat16)
        .transpose(1, 0, 2)
        .reshape(frame_count, local_width)
    )
    branch = lax.psum_scatter(
        jnp.dot(attended, out_weight, preferred_element_type=jnp.float32).astype(jnp.bfloat16),
        "head",
        scatter_dimension=1,
        tiled=True,
    ).astype(jnp.float32)
    encoded = (hidden.astype(jnp.float32) + branch).astype(jnp.bfloat16)
    seq_index = lax.axis_index("seq")
    seq_count = lax.axis_size("seq")
    local_mask = mask_positions - seq_index * frame_count
    masked_full = lax.all_gather(encoded[local_mask], "head", axis=1, tiled=True)
    context = jnp.dot(masked_full, proj_weight, preferred_element_type=jnp.float32)
    masked_count, distract_count = distractors.shape
    request_count = masked_count * distract_count
    capacity = 2 * request_count // seq_count
    target_width = targets.shape[1]
    flat_dist = distractors.reshape(-1)
    owners = flat_dist // frame_count
    row_ids = flat_dist % frame_count
    owner_hits = (owners[:, None] == jnp.arange(seq_count, dtype=jnp.int32)[None, :]).astype(
        jnp.int32
    )
    earlier = jnp.cumsum(owner_hits, axis=0) - owner_hits
    slot_ids = jnp.sum(earlier * owner_hits, axis=1)
    buckets = owners * capacity + slot_ids
    requests = (
        jnp.full((seq_count * capacity,), -1, jnp.int32)
        .at[buckets]
        .set(row_ids)
        .reshape(seq_count, capacity)
    )
    positive = targets[local_mask]
    asked = lax.all_to_all(requests, "seq", split_axis=0, concat_axis=0, tiled=True)
    found = take_rows(asked, targets)
    returned = lax.all_to_all(found, "seq", split_axis=0, concat_axis=0, tiled=True)
    fetched = returned.reshape(seq_count * capacity, target_width)[buckets].reshape(
        masked_count, distract_count, target_width
    )
    cands = jnp.concatenate([positive[:, None, :], fetched], axis=1).astype(jnp.float32)
    products_here = jnp.einsum("me,mke->mk", context, cands, precision=lax.Precision.HIGHEST)
    target_sq_here = jnp.sum(cands * cands, axis=2)
    context_sq_here = jnp.sum(context * context, axis=1)
    products, target_sq, context_sq = lax.psum(
        (products_here, target_sq_here, context_sq_here), "head"
    )
    along, shrink, spread = contrast_terms(products, target_sq, context_sq, loss_weight)
    cand_grads = along[:, :, None] * context[:, None, :] - shrink[:, :, None] * cands
    context_grad = (
        jnp.einsum("mk,mke->me", along, cands, precision=lax.Precision.HIGHEST)
        - spread[:, None] * context
    )
    target_grad = (
        jnp.zeros((frame_count, target_width), jnp.float32).at[local_mask].add(cand_grads[:, 0])
    )
    outgoing = (
        jnp.zeros((seq_count * capacity, target_width), jnp.float32)
        .at[buckets]
        .set(cand_grads[:, 1:].reshape(request_count, target_width))
    )
    incoming = (
        lax.all_to_all(
            outgoing.reshape(seq_count, capacity, target_width).astype(jnp.bfloat16),
            "seq",
            split_axis=0,
            concat_axis=0,
            tiled=True,
        )
        .astype(jnp.float32)
        .reshape(seq_count * capacity, target_width)
    )
    target_grad = target_grad + place_rows(asked.reshape(-1), incoming, frame_count)
    proj_term = jnp.einsum(
        "mw,me->we", masked_full.astype(jnp.float32), context_grad, precision=lax.Precision.HIGHEST
    )
    proj_grad = lax.psum(proj_term, "seq")
    return (encoded, proj_grad, target_grad)


def solution(mesh):
    return jax.shard_map(
        per_device,
        mesh=mesh,
        in_specs=(
            P("seq", "head"),
            P("head", None, None),
            P(),
            P(),
            P("head", None),
            P("head", None),
            P("head", None),
            P("head", None),
            P(None, "head"),
            P("seq", "head"),
            P("seq"),
            P("seq", None),
            P("seq"),
        ),
        out_specs=(P("seq", "head"), P(None, "head"), P("seq", "head")),
        check_vma=False,
    )
```

profile of v0, /device:TPU:8, one launch (start us, length us, event | category | flops | bytes accessed | tf_op | source)
XLA Modules:
  0.0 1307.5 jit_solution(7271690625776360250)
XLA Ops:
  7.2 1.0 fusion.66
  8.2 3.4 collective-permute-start
  11.6 3.3 collective-permute-start.1
  15.0 10.7 copy.41
  25.7 1.3 reshape.245
  27.6 17.3 %fusion.67 = f32[1,129,2,120]{3,0,2,1:T(1,128)S(1)} fusion(bf16[1,256,2,120]{3,0,2,1:T(2,128)(2,1)S(1)} %copy.40, bf16[2,120,120,128]{2,1,0,3:T(8,128)(2,1)} %copy.41), kind=kOutput, calls=%fused_computation.135 | convolution fusion | flops 951091200 | bytes 7619520 | tf_op jit(solution)/shard_map/conv_general_dilated | solution.py:108
  45.3 7.2 all_gather.12
  53.4 0.6 convert_element_type.65
  54.3 1.3 reshape.241
  56.4 0.6 convert_element_type.63
  57.4 18.1 %reduce-window.6 = s32[64,13,128]{2,1,0:T(8,128)S(1)} reduce-window(s32[64,13,128]{2,1,0:T(8,128)S(1)} %reshape.259, s32[]{:T(128)} %constant.57.clone.1), window={size=1x1x128 pad=0_0x0_0x127_0}, to_apply=%region_7.8 | reduce-window | flops 13524992 | bytes 851972 | tf_op jit(solution)/shard_map/reduce-window
  76.7 8.8 scatter_custom_fusion
  85.5 0.7 all_to_all.12
  86.3 12.8 all-to-all-start
  99.1 1.3 reshape.244
  100.6 7.8 all-to-all-done
  109.0 0.8 fusion.64
  110.0 9.9 gather_fusion.2
  119.9 1.5 reshape.279
  121.4 6.3 all-to-all-start.1
  128.5 194.0 %all-gather.7.cloned.1.call-done = bf16[8192,240]{0,1:T(8,128)(2,1)} async-done(((bf16[128,240]{0,1:T(8,128)(2,1)}), bf16[8192,240]{0,1:T(8,128)(2,1)}) %all-gather.7.cloned.1.call-update) | async-done | bytes 3932176 | tf_op jit(solution)/shard_map/all_gather | solution.py:136
  322.5 4.4 copy.77
  326.9 243.4 %all-gather.5.cloned.1.call-done = bf16[8192,240]{0,1:T(8,128)(2,1)} async-done(((bf16[128,240]{0,1:T(8,128)(2,1)}), bf16[8192,240]{0,1:T(8,128)(2,1)}) %all-gather.5.cloned.1.call-update) | async-done | bytes 3932176 | tf_op jit(solution)/shard_map/all_gather | solution.py:135
  570.3 4.4 copy.78
  574.8 29.4 %while.15 = (s32[]{:T(128)}, f32[2,128,120]{1,2,0:T(8,128)S(1)}, f32[2,128]{1,0:T(2,128)S(1)}, f32[2,128]{1,0:T(2,128)S(1)}, bf16[16,512,240]{1,2,0:T(8,128)(2,1...) while((s32[]{:T(128)}, f32[2,128,120]{1,2,0:T(8,128)S(1)}, ...), condition=%wide.region_5.6_spmd.clone, body=%wide.region_2.5_spmd.clone.sunk | while | flops 63794432 | bytes 3371117 | solution.py:145
  574.8 1.1 constant_dynamic-slice_fusion.3
  576.6 1.1 constant_dynamic-slice_fusion.3
  578.4 1.1 constant_dynamic-slice_fusion.3
  580.3 1.1 constant_dynamic-slice_fusion.3
  582.1 1.1 constant_dynamic-slice_fusion.3
  584.0 1.1 constant_dynamic-slice_fusion.3
  585.8 1.1 constant_dynamic-slice_fusion.3
  587.6 1.1 constant_dynamic-slice_fusion.3
  589.5 1.1 constant_dynamic-slice_fusion.3
  591.3 1.1 constant_dynamic-slice_fusion.3
  593.2 1.1 constant_dynamic-slice_fusion.3
  595.0 1.1 constant_dynamic-slice_fusion.3
  596.8 1.1 constant_dynamic-slice_fusion.3
  598.7 1.1 constant_dynamic-slice_fusion.3
  600.5 1.1 constant_dynamic-slice_fusion.3
  602.4 1.1 constant_dynamic-slice_fusion.3
  604.2 1.0 convolution_convert_fusion
  606.0 2.5 reshape.253
  608.5 5.6 gather_fusion.3
  614.7 20.9 %reduce-scatter.2.cloned.1.call-done = bf16[128,240]{0,1:T(8,128)(2,1)} async-done(((bf16[128,960]{0,1:T(8,128)(2,1)}), bf16[128,240]{0,1:T(8,128)(2,1)}) %reduce-scatter.2.cloned.1.call-update) | async-done | bytes 61456 | tf_op jit(solution)/shard_map/reduce_scatter | solution.py:160
  635.6 0.8 add_convert_fusion
  637.1 6.7 all-gather.1
  644.3 0.8 fusion.45
  645.1 13.6 %all-reduce.1 = (f32[16,101]{1,0:T(8,128)S(1)}, f32[16]{0:T(128)S(1)}, f32[16,101]{1,0:T(8,128)S(1)}) all-reduce(f32[16,101]{1,0:T(8,128)S(1)} %fusion.7, f32[16]{0:T(128)S(1)} %get-tuple-element.115, f32[16,101]{1,0:T(8,128)S(1)} %bitcast.173), channel_id=1, replica_groups=mesh['seq'=64,'head'=4] {'head'}, use_global_device_ids=true, to_apply=%region_15.16 | all-reduce | flops 3248 | bytes 25984 | tf_op jit(solution)/shard_map/psum | solution.py:202
  659.0 0.7 fusion.8
  659.7 1.2 copy-done.2
  661.0 1.4 reshape.306
  662.4 12.8 scatter_custom_fusion.1
  675.2 2.1 convert_element_type.73
  677.3 1.5 convert_element_type.74
  678.8 11.5 all-to-all-start.2
  691.2 1.6 fusion.43
  692.9 0.9 slice.50
  693.8 40.9 %all-to-all-done.2 = bf16[64,50,256]{2,1,0:T(8,128)(2,1)S(1)} async-done(((bf16[64,50,256]{2,1,0:T(8,128)(2,1)}), bf16[64,50,256]{2,1,0:T(8,128)(2,1)S(1)}, u32[]{:S(2)}, u32[]{:S(2)}) %all-to-all-start.2) | async-done | bytes 1638432 | tf_op jit(solution)/shard_map/all_to_all | solution.py:220
  734.8 1.9 reshape.314
  736.7 20.7 %scatter_custom_fusion.2 = f32[129,256]{1,0:T(8,128)S(1)} fusion(s32[3200]{0:T(1024)S(1)} %fusion.48, f32[3200,256]{1,0:T(8,128)} %reshape.314, f32[]{:T(128)} %constant.68.clone.1), kind=kCustom, calls=%fused_computation.78 | custom fusion | flops 819200 | bytes 132608 | tf_op jit(solution)/shard_map/scatter-add | solution.py:86
  757.4 0.8 scatter_custom_fusion.3
  758.1 540.6 %all-reduce.4.cloned.1.call-done = f32[960,256]{1,0:T(8,128)} async-done(((f32[960,256]{1,0:T(8,128)}), f32[960,256]{1,0:T(8,128)}) %all-reduce.4.cloned.1.call-update) | async-done | bytes 983056 | tf_op jit(solution)/shard_map/psum | solution.py:234
  1298.8 2.2 copy.94
  (194 shorter events, 21.0 us)
Async XLA Ops:
  7.2 597.1 %copy-start = (bf16[240,960]{1,0:T(8,128)(2,1)S(1)}, bf16[240,960]{1,0:T(8,128)(2,1)}, u32[]{:S(2)}) copy-start(bf16[240,960]{1,0:T(8,128)(2,1)} %param.22) | copy-start | bytes 1382404
  7.2 315.4 %all-gather.7.cloned.1.call-start = ((), (), s32[]{:S(2)}) async-start(), calls=%async_computation.5 | async-start | bytes 3993600 | tf_op jit(solution)/shard_map/all_gather | solution.py:136
  8.2 19.0 %collective-permute-start = (bf16[64,240]{0,1:T(8,128)(2,1)S(1)}, bf16[64,240]{0,1:T(8,128)(2,1)S(1)}, u32[]{:S(2)}, u32[]{:S(2)}) collective-permute-start(bf16[64,240]{0,1:T(8,128)(2,1)S(1)} %get-tuple-element.106), channel_id=1, source_target_pairs={{0,4},{4,8},{8,12},{12,16},{16,20},{20,24},{24,28},{28,32},{32,36}... | collective-permute-start | bytes 92168 | tf_op jit(solution)/shard_map/ppermute | solution.py:20
  11.6 15.6 %collective-permute-start.1 = (bf16[64,240]{0,1:T(8,128)(2,1)S(1)}, bf16[64,240]{0,1:T(8,128)(2,1)S(1)}, u32[]{:S(2)}, u32[]{:S(2)}) collective-permute-start(bf16[64,240]{0,1:T(8,128)(2,1)S(1)} %get-tuple-element.107), channel_id=1, source_target_pairs={{4,0},{8,4},{12,8},{16,12},{20,16},{24,20},{28,24},{32,28},{36,32}... | collective-permute-start | bytes 92168 | tf_op jit(solution)/shard_map/ppermute | solution.py:21
  15.0 10.8 copy-start.5
  25.7 1.5 copy-start.3
  27.6 25.3 %copy-start.12 = (f32[960]{0:T(1024)S(1)}, f32[960]{0:T(1024)}, u32[]{:S(2)}) copy-start(f32[960]{0:T(1024)} %param.18) | copy-start | bytes 11524
  27.6 25.3 %copy-start.13 = (f32[960]{0:T(1024)S(1)}, f32[960]{0:T(1024)}, u32[]{:S(2)}) copy-start(f32[960]{0:T(1024)} %param.17) | copy-start | bytes 11524
  44.9 9.4 copy-start.6
  54.1 3.0 copy-start.10
  54.1 516.2 %all-gather.5.cloned.1.call-start = ((), (), s32[]{:S(2)}) async-start(), calls=%async_computation.4 | async-start | bytes 3993600 | tf_op jit(solution)/shard_map/all_gather | solution.py:135
  75.8 23.3 %copy-start.7 = (bf16[2,115200]{1,0:T(2,128)(2,1)S(1)}, bf16[2,115200]{1,0:T(2,128)(2,1)}, u32[]{:S(2)}) copy-start(bf16[2,115200]{1,0:T(2,128)(2,1)} %param.19) | copy-start | bytes 1382404
  76.4 33.5 %copy-start.1 = (bf16[128,256]{1,0:T(8,128)(2,1)S(1)}, bf16[128,256]{1,0:T(8,128)(2,1)}, u32[]{:S(2)}) copy-start(bf16[128,256]{1,0:T(8,128)(2,1)} %param.24) | copy-start | bytes 196612
  86.3 22.2 %all-to-all-start = ((s32[64,1,50]{2,1,0:T(1,128)}), s32[64,1,50]{2,1,0:T(1,128)S(1)}, u32[]{:S(2)}, u32[]{:S(2)}) async-start(s32[64,1,50]{2,1,0:T(1,128)} %bitcast.24), calls=%async_computation.1 | async-start | bytes 65536 | tf_op jit(solution)/shard_map/all_to_all | solution.py:192
  121.4 484.6 %all-to-all-start.1 = ((bf16[64,50,256]{2,1,0:T(8,128)(2,1)}), bf16[64,50,256]{2,1,0:T(8,128)(2,1)}, u32[]{:S(2)}, u32[]{:S(2)}) async-start(bf16[64,50,256]{2,1,0:T(8,128)(2,1)} %reshape.279), calls=%async_computation.2 | async-start | bytes 3670016 | tf_op jit(solution)/shard_map/all_to_all | solution.py:194
  127.7 507.9 %reduce-scatter.2.cloned.1.call-start = ((), (), s32[]{:S(2)}) async-start(), calls=%async_computation.6 | async-start | bytes 307200 | tf_op jit(solution)/shard_map/reduce_scatter | solution.py:160
  574.8 30.6 %copy-start.14 = (s32[16]{0:T(128)S(1)}, s32[16]{0:T(128)}, u32[]{:S(2)}) copy-start(s32[16]{0:T(128)} %param.25) | copy-start | bytes 196
  614.1 29.9 %copy-start.4 = (bf16[960,256]{1,0:T(8,128)(2,1)S(1)}, bf16[960,256]{1,0:T(8,128)(2,1)}, u32[]{:S(2)}) copy-start(bf16[960,256]{1,0:T(8,128)(2,1)} %param.23) | copy-start | bytes 1474564
  614.3 44.5 %copy-start.11 = (f32[16]{0:T(128)S(1)}, f32[16]{0:T(128)}, u32[]{:S(2)}) copy-start(f32[16]{0:T(128)} %param.27) | copy-start | bytes 196
  636.4 23.3 %copy-start.8 = (bf16[128,240]{0,1:T(8,128)(2,1)}, bf16[128,240]{0,1:T(8,128)(2,1)S(1)}, u32[]{:S(2)}) copy-start(bf16[128,240]{0,1:T(8,128)(2,1)S(1)} %add_convert_fusion) | copy-start | bytes 184324
  659.7 1.2 copy-start.2
  678.8 56.0 %all-to-all-start.2 = ((bf16[64,50,256]{2,1,0:T(8,128)(2,1)}), bf16[64,50,256]{2,1,0:T(8,128)(2,1)S(1)}, u32[]{:S(2)}, u32[]{:S(2)}) async-start(bf16[64,50,256]{2,1,0:T(8,128)(2,1)} %convert_element_type.74), calls=%async_computation.3 | async-start | bytes 3670016 | tf_op jit(solution)/shard_map/all_to_all | solution.py:220
  690.2 608.5 %all-reduce.4.cloned.1.call-start = ((), (), s32[]{:S(2)}) async-start(), calls=%async_computation.7 | async-start | bytes 1966080 | tf_op jit(solution)/shard_map/psum | solution.py:234
  758.1 542.8 %copy-start.9 = (f32[128,256]{1,0:T(8,128)}, f32[128,256]{1,0:T(8,128)S(1)}, u32[]{:S(2)}) copy-start(f32[128,256]{1,0:T(8,128)S(1)} %scatter_custom_fusion.3) | copy-start | bytes 393220
Sparse Core Ops, SparseCore 0:
  54.2 268.2 all-gather.6
  324.8 245.4 all-gather.4
  605.4 30.1 reduce-scatter.1
  694.2 604.5 all-reduce.3
where the time goes:
time: 1310 us
  waiting for transfers between devices  1050 us (80%)
  local copies, waits for them, and re-layouts  97.4 us (7%)
  other arithmetic  49.3 us (4%)
  starting transfers between devices  38.1 us (3%)
  matrix products  32.3 us (2%)
  blocking collectives  27.5 us (2%)
  between operations  14.4 us (1%)
    psum x1, waiting for transfers between devices, per_device(): proj_grad = lax.psum(proj_term, 'seq')  541 us
    all_gather x1, waiting for transfers between devices, per_device(): key_piece = lax.all_gather(key_here, 'seq', axis=0, tiled=True)  243 us
    all_gather x1, waiting for transfers between devices, per_device(): value_piece = lax.all_gather(value_here, 'seq', axis=0, tiled=True)  194 us
    all_to_all x1, waiting for transfers between devices, per_device(): lax.all_to_all(outgoing.reshape(seq_count, capacity, target_width).astype...  40.9 us
  transfers between devices with their start and end apart: 9, of which 6 were waited for; matrix products, arithmetic and copies ran while one was open for 10% of the time, Pallas kernels for 0%

commit v1 on v0

--- a/solution.py
+++ b/solution.py
@@ -231,7 +231,8 @@
     proj_term = jnp.einsum(
         "mw,me->we", masked_full.astype(jnp.float32), context_grad, precision=lax.Precision.HIGHEST
     )
-    proj_grad = lax.psum(proj_term, "seq")
+    pieces = lax.all_gather(proj_term, "seq")
+    proj_grad = jnp.sum(pieces, axis=0)
     return (encoded, proj_grad, target_grad)
 
 

time: 1310 us -> 2060 us (1.57)
  waiting for transfers between devices: 1050 us -> 1770 us
    all_gather x0 -> x1, waiting for transfers between devices: none -> 1250 us  [per_device(): pieces = lax.all_gather(proj_term, 'seq')]
    psum x1 -> x0, waiting for transfers between devices: 541 us -> none  [per_device(): proj_grad = lax.psum(proj_term, 'seq')]
  transfers between devices with their start and end apart: 9 -> 9, of which waited for: 6 -> 6; matrix products, arithmetic and copies ran while one was open for 10% -> 7% of each run, Pallas kernels for 0% -> 0%
where the time goes in v1:
time: 2060 us; the launch traced here: 2050 us
  waiting for transfers between devices  1770 us (86%)
  local copies, waits for them, and re-layouts  96.2 us (5%)
  other arithmetic  69.8 us (3%)
  starting transfers between devices  38 us (2%)
  matrix products  32.3 us (2%)
  blocking collectives  27.5 us (1%)
    all_gather x1, waiting for transfers between devices, per_device(): pieces = lax.all_gather(proj_term, 'seq')  1250 us
    all_gather x1, waiting for transfers between devices, per_device(): key_piece = lax.all_gather(key_here, 'seq', axis=0, tiled=True)  245 us
    all_gather x1, waiting for transfers between devices, per_device(): value_piece = lax.all_gather(value_here, 'seq', axis=0, tiled=True)  192 us
    all_to_all x1, waiting for transfers between devices, per_device(): lax.all_to_all(outgoing.reshape(seq_count, capacity, target_width).astype...  54.9 us
  transfers between devices with their start and end apart: 9, of which 6 were waited for; matrix products, arithmetic and copies ran while one was open for 7% of the time, Pallas kernels for 0%

profile of v1, /device:TPU:8, one launch (start us, length us, event | category | flops | bytes accessed | tf_op | source)
XLA Modules:
  0.0 2053.6 jit_solution(4974644809966801104)
XLA Ops:
  7.2 1.0 fusion.66
  8.2 3.4 collective-permute-start
  11.6 3.3 collective-permute-start.1
  15.0 10.7 copy.41
  25.7 1.3 reshape.245
  27.6 17.3 fusion.67
  45.3 7.2 all_gather.18
  54.3 1.3 reshape.241
  56.4 0.6 convert_element_type.63
  57.4 18.1 reduce-window.6
  76.7 8.8 scatter_custom_fusion
  85.5 0.7 all_to_all.12
  86.3 12.8 all-to-all-start
  99.1 1.3 reshape.244
  100.4 1.0 copy.44
  101.4 7.1 all-to-all-done
  109.1 0.8 fusion.64
  110.0 9.9 gather_fusion.2
  120.0 1.5 reshape.279
  121.4 6.5 all-to-all-start.1
  128.5 192.1 %all-gather.9.cloned.1.call-done = bf16[8192,240]{0,1:T(8,128)(2,1)} async-done(((bf16[128,240]{0,1:T(8,128)(2,1)}), bf16[8192,240]{0,1:T(8,128)(2,1)}) %all-gather.9.cloned.1.call-update) | async-done | bytes 3932176 | tf_op jit(solution)/shard_map/all_gather | solution.py:136
  320.7 4.4 copy.77
  325.1 245.5 %all-gather.7.cloned.1.call-done = bf16[8192,240]{0,1:T(8,128)(2,1)} async-done(((bf16[128,240]{0,1:T(8,128)(2,1)}), bf16[8192,240]{0,1:T(8,128)(2,1)}) %all-gather.7.cloned.1.call-update) | async-done | bytes 3932176 | tf_op jit(solution)/shard_map/all_gather | solution.py:135
  570.5 4.5 copy.78
  575.1 29.4 %while.15 = (s32[]{:T(128)}, f32[2,128,120]{1,2,0:T(8,128)S(1)}, f32[2,128]{1,0:T(2,128)S(1)}, f32[2,128]{1,0:T(2,128)S(1)}, bf16[16,512,240]{1,2,0:T(8,128)(2,1...) while((s32[]{:T(128)}, f32[2,128,120]{1,2,0:T(8,128)S(1)}, ...), condition=%wide.region_5.6_spmd.clone, body=%wide.region_2.5_spmd.clone.sunk | while | flops 63794432 | bytes 3371117 | solution.py:145
  575.1 1.1 constant_dynamic-slice_fusion.3
  576.9 1.1 constant_dynamic-slice_fusion.3
  578.7 1.1 constant_dynamic-slice_fusion.3
  580.6 1.1 constant_dynamic-slice_fusion.3
  582.4 1.1 constant_dynamic-slice_fusion.3
  584.3 1.1 constant_dynamic-slice_fusion.3
  586.1 1.1 constant_dynamic-slice_fusion.3
  587.9 1.1 constant_dynamic-slice_fusion.3
  589.8 1.1 constant_dynamic-slice_fusion.3
  591.6 1.1 constant_dynamic-slice_fusion.3
  593.5 1.1 constant_dynamic-slice_fusion.3
  595.3 1.1 constant_dynamic-slice_fusion.3
  597.1 1.1 constant_dynamic-slice_fusion.3
  599.0 1.1 constant_dynamic-slice_fusion.3
  600.8 1.1 constant_dynamic-slice_fusion.3
  602.7 1.1 constant_dynamic-slice_fusion.3
  604.5 1.0 convolution_convert_fusion
  606.6 2.5 reshape.253
  609.1 5.6 gather_fusion.3
  615.3 20.6 %reduce-scatter.2.cloned.1.call-done = bf16[128,240]{0,1:T(8,128)(2,1)} async-done(((bf16[128,960]{0,1:T(8,128)(2,1)}), bf16[128,240]{0,1:T(8,128)(2,1)}) %reduce-scatter.2.cloned.1.call-update) | async-done | bytes 61456 | tf_op jit(solution)/shard_map/reduce_scatter | solution.py:160
  635.9 0.8 add_convert_fusion
  637.4 6.7 all-gather.2
  644.6 0.8 fusion.45
  645.4 13.6 all-reduce.1
  659.9 1.6 fusion.43
  661.5 0.7 fusion.8
  662.2 1.2 copy-done.3
  663.5 1.4 reshape.306
  664.9 12.8 scatter_custom_fusion.1
  677.7 2.1 convert_element_type.73
  679.8 1.5 convert_element_type.74
  681.3 11.5 all-to-all-start.2
  692.9 0.9 slice.50
  693.9 54.9 %all-to-all-done.2 = bf16[64,50,256]{2,1,0:T(8,128)(2,1)S(1)} async-done(((bf16[64,50,256]{2,1,0:T(8,128)(2,1)}), bf16[64,50,256]{2,1,0:T(8,128)(2,1)S(1)}, u32[]{:S(2)}, u32[]{:S(2)}) %all-to-all-start.2) | async-done | bytes 1638432 | tf_op jit(solution)/shard_map/all_to_all | solution.py:220
  748.8 1.9 reshape.314
  750.7 20.7 %scatter_custom_fusion.2 = f32[129,256]{1,0:T(8,128)S(1)} fusion(s32[3200]{0:T(1024)S(1)} %fusion.48, f32[3200,256]{1,0:T(8,128)} %reshape.314, f32[]{:T(128)} %constant.68.clone.1), kind=kCustom, calls=%fused_computation.78 | custom fusion | flops 819200 | bytes 132608 | tf_op jit(solution)/shard_map/scatter-add | solution.py:86
  771.4 0.8 scatter_custom_fusion.3
  772.2 1254.3 %all-gather.11.cloned.1.call-done = f32[61440,256]{1,0:T(8,128)} async-done(((f32[960,256]{1,0:T(8,128)}), f32[61440,256]{1,0:T(8,128)}) %all-gather.11.cloned.1.call-update) | async-done | bytes 62914576 | tf_op jit(solution)/shard_map/all_gather | solution.py:234
  2026.5 20.6 %reduce_sum.91 = f32[960,256]{1,0:T(8,128)} reduce(f32[64,960,256]{2,1,0:T(8,128)} %bitcast.148, f32[]{:T(128)} %constant.68.clone.1), dimensions={0}, to_apply=%region_18.19 | reduce | flops 15482880 | bytes 63897604 | tf_op jit(solution)/shard_map/reduce_sum | solution.py:235
  (198 shorter events, 21.3 us)
Async XLA Ops:
  7.2 597.4 %copy-start = (bf16[240,960]{1,0:T(8,128)(2,1)S(1)}, bf16[240,960]{1,0:T(8,128)(2,1)}, u32[]{:S(2)}) copy-start(bf16[240,960]{1,0:T(8,128)(2,1)} %param.22) | copy-start | bytes 1382404
  7.2 313.5 %all-gather.9.cloned.1.call-start = ((), (), s32[]{:S(2)}) async-start(), calls=%async_computation.5 | async-start | bytes 3993600 | tf_op jit(solution)/shard_map/all_gather | solution.py:136
  8.2 19.0 collective-permute-start
  11.6 15.6 collective-permute-start.1
  15.0 10.8 copy-start.7
  25.7 1.5 copy-start.4
  27.6 25.3 %copy-start.14 = (f32[960]{0:T(1024)S(1)}, f32[960]{0:T(1024)}, u32[]{:S(2)}) copy-start(f32[960]{0:T(1024)} %param.18) | copy-start | bytes 11524
  27.6 25.3 %copy-start.15 = (f32[960]{0:T(1024)S(1)}, f32[960]{0:T(1024)}, u32[]{:S(2)}) copy-start(f32[960]{0:T(1024)} %param.17) | copy-start | bytes 11524
  44.9 9.4 copy-start.8
  54.1 3.0 copy-start.12
  54.1 516.5 %all-gather.7.cloned.1.call-start = ((), (), s32[]{:S(2)}) async-start(), calls=%async_computation.4 | async-start | bytes 3993600 | tf_op jit(solution)/shard_map/all_gather | solution.py:135
  75.8 23.3 %copy-start.9 = (bf16[2,115200]{1,0:T(2,128)(2,1)S(1)}, bf16[2,115200]{1,0:T(2,128)(2,1)}, u32[]{:S(2)}) copy-start(bf16[2,115200]{1,0:T(2,128)(2,1)} %param.19) | copy-start | bytes 1382404
  76.4 33.6 %copy-start.2 = (bf16[128,256]{1,0:T(8,128)(2,1)S(1)}, bf16[128,256]{1,0:T(8,128)(2,1)}, u32[]{:S(2)}) copy-start(bf16[128,256]{1,0:T(8,128)(2,1)} %param.24) | copy-start | bytes 196612
  86.3 22.2 %all-to-all-start = ((s32[64,1,50]{2,1,0:T(1,128)}), s32[64,1,50]{2,1,0:T(1,128)S(1)}, u32[]{:S(2)}, u32[]{:S(2)}) async-start(s32[64,1,50]{2,1,0:T(1,128)} %bitcast.24), calls=%async_computation.1 | async-start | bytes 65536 | tf_op jit(solution)/shard_map/all_to_all | solution.py:192
  121.4 6.5 copy-start.6
  121.4 485.1 %all-to-all-start.1 = ((bf16[64,50,256]{2,1,0:T(8,128)(2,1)}), bf16[64,50,256]{2,1,0:T(8,128)(2,1)}, u32[]{:S(2)}, u32[]{:S(2)}) async-start(bf16[64,50,256]{2,1,0:T(8,128)(2,1)} %reshape.279), calls=%async_computation.2 | async-start | bytes 3670016 | tf_op jit(solution)/shard_map/all_to_all | solution.py:194
  127.9 508.0 %reduce-scatter.2.cloned.1.call-start = ((), (), s32[]{:S(2)}) async-start(), calls=%async_computation.6 | async-start | bytes 307200 | tf_op jit(solution)/shard_map/reduce_scatter | solution.py:160
  575.1 30.8 %copy-start.16 = (s32[16]{0:T(128)S(1)}, s32[16]{0:T(128)}, u32[]{:S(2)}) copy-start(s32[16]{0:T(128)} %param.25) | copy-start | bytes 196
  605.6 1420.8 %all-gather.11.cloned.1.call-start = ((), (), s32[]{:S(2)}) async-start(), calls=%async_computation.7 | async-start | bytes 63897600 | tf_op jit(solution)/shard_map/all_gather | solution.py:234
  614.7 29.6 %copy-start.5 = (bf16[960,256]{1,0:T(8,128)(2,1)S(1)}, bf16[960,256]{1,0:T(8,128)(2,1)}, u32[]{:S(2)}) copy-start(bf16[960,256]{1,0:T(8,128)(2,1)} %param.23) | copy-start | bytes 1474564
  614.8 44.3 %copy-start.13 = (f32[16]{0:T(128)S(1)}, f32[16]{0:T(128)}, u32[]{:S(2)}) copy-start(f32[16]{0:T(128)} %param.27) | copy-start | bytes 196
  636.7 23.2 %copy-start.10 = (bf16[128,240]{0,1:T(8,128)(2,1)}, bf16[128,240]{0,1:T(8,128)(2,1)S(1)}, u32[]{:S(2)}) copy-start(bf16[128,240]{0,1:T(8,128)(2,1)S(1)} %add_convert_fusion) | copy-start | bytes 184324
  662.2 1.2 copy-start.3
  681.3 67.5 %all-to-all-start.2 = ((bf16[64,50,256]{2,1,0:T(8,128)(2,1)}), bf16[64,50,256]{2,1,0:T(8,128)(2,1)S(1)}, u32[]{:S(2)}, u32[]{:S(2)}) async-start(bf16[64,50,256]{2,1,0:T(8,128)(2,1)} %convert_element_type.74), calls=%async_computation.3 | async-start | bytes 3670016 | tf_op jit(solution)/shard_map/all_to_all | solution.py:220
  772.1 1274.9 %copy-start.11 = (f32[128,256]{1,0:T(8,128)}, f32[128,256]{1,0:T(8,128)S(1)}, u32[]{:S(2)}) copy-start(f32[128,256]{1,0:T(8,128)S(1)} %scatter_custom_fusion.3) | copy-start | bytes 393220
  2026.5 20.6 %copy-start.1 = (bf16[240,960]{1,0:T(8,128)(2,1)S(1)}, bf16[240,960]{1,0:T(8,128)(2,1)}, u32[]{:S(2)}) copy-start(bf16[240,960]{1,0:T(8,128)(2,1)} %param.22) | copy-start | bytes 1382404
Sparse Core Ops, SparseCore 0:
  54.2 266.3 all-gather.8
  322.9 247.5 all-gather.6
  605.7 30.1 reduce-scatter.1
  661.6 1364.7 all-gather.10
